TPU v7x, 32 devices: a whole 2x2x4 slice. The times are simulated.
32 devices in a mesh: pipe: 8 (over z, y), tensor: 4 (over x, core).
Axes of the slice: x: 2, y: 2, z: 4, core: 2. Of those that a mesh axis runs over, the one named last changes fastest.
Arguments:
- arriving: float32 [8, 8192, 384], P('pipe', 'tensor'), may hold values from -6 to 6
- stash: bfloat16 [2, 8, 8192, 384], P(None, 'pipe', 'tensor'), may hold values from -6 to 6
- grad_in: float32 [8, 8192, 384], P('pipe', 'tensor'), may hold values from -6 to 6
- first_up: bfloat16 [8, 64, 128, 128], P('pipe', 'tensor'), may hold values from -0.5 to 0.5
- second_up: bfloat16 [8, 128, 64, 256], P('pipe', 'tensor'), may hold values from -0.75 to 0.75
- first_down: bfloat16 [8, 128, 64, 256], P('pipe', 'tensor'), may hold values from -0.375 to 0.375
- second_down: bfloat16 [8, 64, 128, 128], P('pipe', 'tensor'), may hold values from -0.5 to 0.5
Outputs:
- arriving_out: float32 [8, 8192, 384], P('pipe', 'tensor')
- grad_out: float32 [8, 8192, 384], P('pipe', 'tensor')
- first_up_grad: float32 [8, 64, 128, 128], P('pipe', 'tensor')
- second_up_grad: float32 [8, 128, 64, 256], P('pipe', 'tensor')
- first_down_grad: float32 [8, 128, 64, 256], P('pipe', 'tensor')
- second_down_grad: float32 [8, 64, 128, 128], P('pipe', 'tensor')
All inputs are finite; a program needn't handle non-finite values.
Results may differ from a plain program's by a relative error of at most 0.007.
Values may be sent and summed in bfloat16 or wider, within the bound.
No kernel may reach another device: no remote copies, remote signals or barrier semaphores. Data moves between devices by JAX's collectives and lax.ppermute only.
A program may use at most 192 MiB of HBM per device.

v0:
```python
import jax
import jax.numpy as jnp
from jax import lax
from jax.sharding import PartitionSpec as P


def shifted(value, axis, by):
    count = lax.axis_size(axis)
    return lax.ppermute(value, axis, [(i, (i + by) % count) for i in range(count)])


def smooth(values):
    return jax.nn.gelu(values, approximate=True)


def to_columns(value):
    return lax.all_to_all(value, "tensor", split_axis=1, concat_axis=0, tiled=True)


def to_rows(value):
    return lax.all_to_all(value, "tensor", split_axis=0, concat_axis=1, tiled=True)


def front(narrow_in, first_up, second_up, first_down):
    first_out = jnp.einsum(
        "njr,nji->nir", narrow_in, first_up, preferred_element_type=jnp.float32
    ).astype(jnp.bfloat16)
    spread = to_columns(first_out)
    hidden_pre = jnp.einsum("nir,inf->ifr", spread, second_up, preferred_element_type=jnp.float32)
    hidden = smooth(hidden_pre).astype(jnp.bfloat16)
    local_fold = jnp.einsum(
        "ifr,inf->nir", hidden, first_down, preferred_element_type=jnp.float32
    ).astype(jnp.bfloat16)
    folded = to_rows(local_fold)
    return (spread, hidden_pre, hidden, folded)


def backward(narrow_in, cotangent, first_up, second_up, first_down, second_down, parts):
    spread, hidden_pre, hidden, folded = parts
    narrow_grad = cotangent.astype(jnp.bfloat16).reshape(narrow_in.shape)
    grad_second_down = jnp.einsum(
        "nir,nkr->nik", folded, narrow_grad, preferred_element_type=jnp.float32
    )
    local_grad = jnp.einsum(
        "nkr,nik->nir", narrow_grad, second_down, preferred_element_type=jnp.float32
    ).astype(jnp.bfloat16)
    grad_folded = to_columns(local_grad)
    grad_first_down = jnp.einsum(
        "ifr,nir->inf", hidden, grad_folded, preferred_element_type=jnp.float32
    )
    grad_hidden = jnp.einsum(
        "nir,inf->ifr", grad_folded, first_down, preferred_element_type=jnp.float32
    )
    smooth_back = jax.vjp(smooth, hidden_pre)[1]
    grad_pre = smooth_back(grad_hidden)[0].astype(jnp.bfloat16)
    grad_second_up = jnp.einsum(
        "nir,ifr->inf", spread, grad_pre, preferred_element_type=jnp.float32
    )
    column_grad = jnp.einsum(
        "ifr,inf->nir", grad_pre, second_up, preferred_element_type=jnp.float32
    ).astype(jnp.bfloat16)
    grad_first = to_rows(column_grad)
    grad_first_up = jnp.einsum(
        "njr,nir->nji", narrow_in, grad_first, preferred_element_type=jnp.float32
    )
    grad_input = jnp.einsum(
        "nir,nji->njr", grad_first, first_up, preferred_element_type=jnp.float32
    ).reshape(cotangent.shape)
    return (grad_input, (grad_first_up, grad_second_up, grad_first_down, grad_second_down))


def body(arriving, stash, grad_in, first_up, second_up, first_down, second_down):
    activation = arriving[0]
    cotangent = grad_in[0]
    up_first = first_up[0]
    up_second = second_up[0]
    down_first = first_down[0]
    down_second = second_down[0]
    blocks = up_first.shape[0]
    width = up_first.shape[1]
    rows = activation.shape[1]
    far_activation = shifted(activation, "pipe", 2)
    far_cotangent = shifted(cotangent, "pipe", -2)
    current = activation.astype(jnp.bfloat16).reshape(blocks, width, rows)
    folded_ahead = front(current, up_first, up_second, down_first)[3]
    step = jnp.einsum(
        "nir,nik->nkr", folded_ahead, down_second, preferred_element_type=jnp.float32
    ).reshape(activation.shape)
    output = activation + step
    near_activation = shifted(output.astype(jnp.bfloat16), "pipe", 1)
    step, cotangent = lax.optimization_barrier((step, cotangent))
    stored = stash[0, 0].reshape(blocks, width, rows)
    behind = front(stored, up_first, up_second, down_first)
    grad_step, totals = backward(
        stored, cotangent, up_first, up_second, down_first, down_second, behind
    )
    grad_input = cotangent + grad_step
    near_cotangent = shifted(grad_input.astype(jnp.bfloat16), "pipe", -1)
    step, grad_step, far_activation, far_cotangent = lax.optimization_barrier(
        (step, grad_step, far_activation, far_cotangent)
    )
    far_step = shifted(step.astype(jnp.bfloat16), "pipe", 2)
    far_grad_step = shifted(grad_step.astype(jnp.bfloat16), "pipe", -2)
    current = near_activation.reshape(blocks, width, rows)
    folded_ahead = front(current, up_first, up_second, down_first)[3]
    step = jnp.einsum(
        "nir,nik->nkr", folded_ahead, down_second, preferred_element_type=jnp.float32
    ).reshape(activation.shape)
    last_step = shifted(step.astype(jnp.bfloat16), "pipe", 1)
    step, near_cotangent, far_step, far_grad_step = lax.optimization_barrier(
        (step, near_cotangent, far_step, far_grad_step)
    )
    stored = stash[1, 0].reshape(blocks, width, rows)
    behind = front(stored, up_first, up_second, down_first)
    grad_step, terms = backward(
        stored, near_cotangent, up_first, up_second, down_first, down_second, behind
    )
    last_grad_step = shifted(grad_step.astype(jnp.bfloat16), "pipe", -1)
    activation = far_activation + (far_step.astype(jnp.float32) + last_step.astype(jnp.float32))
    cotangent = far_cotangent + (
        far_grad_step.astype(jnp.float32) + last_grad_step.astype(jnp.float32)
    )
    totals = (
        totals[0] + terms[0],
        totals[1] + terms[1],
        totals[2] + terms[2],
        totals[3] + terms[3],
    )
    return (
        activation[None],
        cotangent[None],
        totals[0][None],
        totals[1][None],
        totals[2][None],
        totals[3][None],
    )


def solution(mesh):
    placed = (
        P("pipe", "tensor", None),
        P(None, "pipe", "tensor", None),
        P("pipe", "tensor", None),
        P("pipe", "tensor", None, None),
        P("pipe", "tensor", None, None),
        P("pipe", "tensor", None, None),
        P("pipe", "tensor", None, None),
    )
    return jax.shard_map(
        body,
        mesh=mesh,
        in_specs=placed,
        out_specs=(
            P("pipe", "tensor", None),
            P("pipe", "tensor", None),
            P("pipe", "tensor", None, None),
            P("pipe", "tensor", None, None),
            P("pipe", "tensor", None, None),
            P("pipe", "tensor", None, None),
        ),
        check_vma=False,
    )
```

profile of v0, /device:TPU:0, one launch (start us, length us, event | category | flops | bytes accessed | tf_op | source)
XLA Modules:
  0.0 497.8 jit_solution(13819847129199727905)
XLA Ops:
  16.0 14.7 %all-to-all-done = bf16[16,128,384]{2,0,1:T(8,128)(2,1)} async-done(((bf16[16,128,384]{2,0,1:T(8,128)(2,1)}), bf16[16,128,384]{2,0,1:T(8,128)(2,1)}, u32[]{:S(2)}, u32[]{:S(2)}) %all-to-all-start) | async-done | bytes 1572896 | tf_op jit(solution)/shard_map/all_to_all | solution.py:17
  37.8 7.6 %fusion.55 = bf16[64,32,384]{2,0,1:T(8,128)(2,1)} fusion(bf16[64,32,384]{2,0,1:T(8,128)(2,1)} %bitcast.292, bf16[1,32,64,256]{3,2,1,0:T(8,128)(2,1)} %param.12, bf16[1,32,64,256]{3,2,1,0:T(8,128)(2,1)S(1)} %copy-done), kind=kOutput, calls=%fused_computation.74 | convolution fusion | flops 834404352 | bytes 5242880 | tf_op jit(solution)/shard_map/ifr,inf->nir/dot_general | solution.py:31
  48.9 6.2 %all-to-all-done.8 = bf16[16,128,384]{2,0,1:T(8,128)(2,1)} async-done(((bf16[16,128,384]{2,0,1:T(8,128)(2,1)}), bf16[16,128,384]{2,0,1:T(8,128)(2,1)}, u32[]{:S(2)}, u32[]{:S(2)}) %all-to-all-start.8) | async-done | bytes 1572896 | tf_op jit(solution)/shard_map/all_to_all | solution.py:17
  62.2 17.4 %all-to-all-done.1 = bf16[64,32,384]{2,1,0:T(8,128)(2,1)} async-done(((bf16[64,32,384]{2,1,0:T(8,128)(2,1)}), bf16[64,32,384]{2,1,0:T(8,128)(2,1)}, u32[]{:S(2)}, u32[]{:S(2)}) %all-to-all-start.1) | async-done | bytes 1572896 | tf_op jit(solution)/shard_map/all_to_all | solution.py:21
  108.7 6.4 %fusion.74 = f32[32,384,256]{2,1,0:T(8,128)} fusion(bf16[64,32,384]{2,0,1:T(8,128)(2,1)S(1)} %bitcast.273, bf16[1,32,64,256]{3,2,1,0:T(8,128)(2,1)S(1)} %copy-done), kind=kOutput, calls=%fused_computation.93 | convolution fusion | flops 402653184 | bytes 15204352 | tf_op jit(solution)/shard_map/nir,inf->ifr/dot_general | solution.py:29
  118.0 8.6 %fusion.34 = (bf16[32,256,384]{1,2,0:T(8,128)(2,1)}, f32[32,384,256]{2,1,0:T(8,128)}) fusion(bf16[64,32,384]{2,0,1:T(8,128)(2,1)S(1)} %bitcast.281, bf16[1,32,64,256]{3,2,1,0:T(8,128)(2,1)S(1)} %copy-done), kind=kOutput, calls=%fused_computation.45 | convolution fusion | flops 430964736 | bytes 21495808 | tf_op jit(solution)/shard_map/nir,inf->ifr/dot_general | solution.py:29
  130.6 12.2 %fusion.6 = bf16[32,256,384]{1,2,0:T(8,128)(2,1)S(1)} fusion(f32[32,384,256]{2,1,0:T(8,128)} %get-tuple-element.45, bf16[64,32,384]{2,0,1:T(8,128)(2,1)S(1)} %bitcast.283, bf16[1,32,64,256]{3,2,1,0:T(8,128)(2,1)S(1)} %copy-done.28), kind=kOutput, calls=%fused_computation.12 | convolution fusion | flops 465567744 | bytes 21495808 | tf_op jit(solution)/shard_map/nir,inf->ifr/dot_general | solution.py:51
  147.4 4.6 all-to-all-start.4
  152.0 7.9 %fusion.61 = bf16[64,32,384]{2,0,1:T(8,128)(2,1)S(1)} fusion(bf16[1,32,64,256]{3,2,1,0:T(8,128)(2,1)S(1)} %copy-done.28, f32[32,384,256]{2,1,0:T(8,128)} %fusion.74), kind=kOutput, calls=%fused_computation.78 | convolution fusion | flops 431751168 | bytes 15204352 | tf_op jit(solution)/shard_map/ifr,inf->nir/dot_general | solution.py:31
  162.0 10.1 %all-to-all-done.4 = bf16[64,32,384]{2,1,0:T(8,128)(2,1)} async-done(((bf16[64,32,384]{2,1,0:T(8,128)(2,1)}), bf16[64,32,384]{2,1,0:T(8,128)(2,1)}, u32[]{:S(2)}, u32[]{:S(2)}) %all-to-all-start.4) | async-done | bytes 1572896 | tf_op jit(solution)/shard_map/all_to_all | solution.py:21
  189.8 35.5 %collective-permute-done = f32[2048,384]{1,0:T(8,128)} collective-permute-done((f32[2048,384]{1,0:T(8,128)}, f32[2048,384]{1,0:T(8,128)}, u32[]{:S(2)}, u32[]{:S(2)}) %collective-permute-start) | collective-permute-done | bytes 3145760 | tf_op jit(solution)/shard_map/ppermute | solution.py:9
  242.2 18.3 %collective-permute-done.2 = bf16[2048,384]{1,0:T(8,128)(2,1)} collective-permute-done((bf16[2048,384]{1,0:T(8,128)(2,1)}, bf16[2048,384]{1,0:T(8,128)(2,1)}, u32[]{:S(2)}, u32[]{:S(2)}) %collective-permute-start.2) | collective-permute-done | bytes 1572896 | tf_op jit(solution)/shard_map/ppermute | solution.py:9
  277.4 16.2 %collective-permute-done.3 = bf16[2048,384]{1,0:T(8,128)(2,1)} collective-permute-done((bf16[2048,384]{1,0:T(8,128)(2,1)}, bf16[2048,384]{1,0:T(8,128)(2,1)}, u32[]{:S(2)}, u32[]{:S(2)}) %collective-permute-start.3) | collective-permute-done | bytes 1572896 | tf_op jit(solution)/shard_map/ppermute | solution.py:9
  293.7 15.2 %collective-permute-done.5 = bf16[2048,384]{1,0:T(8,128)(2,1)} collective-permute-done((bf16[2048,384]{1,0:T(8,128)(2,1)}, bf16[2048,384]{1,0:T(8,128)(2,1)}, u32[]{:S(2)}, u32[]{:S(2)}) %collective-permute-start.5) | collective-permute-done | bytes 1572896 | tf_op jit(solution)/shard_map/ppermute | solution.py:9
  308.9 34.2 %collective-permute-done.4 = bf16[2048,384]{1,0:T(8,128)(2,1)} collective-permute-done((bf16[2048,384]{1,0:T(8,128)(2,1)}, bf16[2048,384]{1,0:T(8,128)(2,1)}, u32[]{:S(2)}, u32[]{:S(2)}) %collective-permute-start.4) | collective-permute-done | bytes 1572896 | tf_op jit(solution)/shard_map/ppermute | solution.py:9
  349.2 4.8 all-to-all-start.7
  354.0 5.8 %fusion.109 = f32[32,64,256]{2,1,0:T(8,128)} fusion(bf16[64,32,384]{2,0,1:T(8,128)(2,1)} %bitcast.284, bf16[32,256,384]{1,2,0:T(8,128)(2,1)} %get-tuple-element.44), kind=kOutput, calls=%fused_computation.125 | convolution fusion | flops 402653184 | bytes 9961472 | tf_op jit(solution)/shard_map/ifr,nir->inf/dot_general | solution.py:48
  362.7 7.6 %fusion.52 = bf16[64,32,384]{2,0,1:T(8,128)(2,1)} fusion(bf16[64,32,384]{2,0,1:T(8,128)(2,1)} %bitcast.293, bf16[1,32,64,256]{3,2,1,0:T(8,128)(2,1)} %param.12, bf16[1,32,64,256]{3,2,1,0:T(8,128)(2,1)S(1)} %copy-done), kind=kOutput, calls=%fused_computation.73 | convolution fusion | flops 834404352 | bytes 5242880 | tf_op jit(solution)/shard_map/ifr,inf->nir/dot_general | solution.py:31
  380.5 12.2 %fusion.13 = bf16[32,256,384]{1,2,0:T(8,128)(2,1)S(1)} fusion(f32[32,384,256]{2,1,0:T(8,128)} %fusion.74, bf16[64,32,384]{2,0,1:T(8,128)(2,1)S(1)} %bitcast.290, bf16[1,32,64,256]{3,2,1,0:T(8,128)(2,1)S(1)} %copy-done.30), kind=kOutput, calls=%fused_computation.19 | convolution fusion | flops 465567744 | bytes 21495808 | tf_op jit(solution)/shard_map/nir,inf->ifr/dot_general | solution.py:51
  403.2 5.9 %fusion.108 = f32[32,64,256]{2,1,0:T(8,128)} fusion(bf16[64,32,384]{2,0,1:T(8,128)(2,1)} %bitcast.282, bf16[32,256,384]{1,2,0:T(8,128)(2,1)} %copy-done.3), kind=kOutput, calls=%fused_computation.124 | convolution fusion | flops 402653184 | bytes 9961472 | tf_op jit(solution)/shard_map/nir,ifr->inf/dot_general | solution.py:56
  417.6 5.7 %all-to-all-done.9 = bf16[64,32,384]{2,1,0:T(8,128)(2,1)} async-done(((bf16[64,32,384]{2,1,0:T(8,128)(2,1)}), bf16[64,32,384]{2,1,0:T(8,128)(2,1)}, u32[]{:S(2)}, u32[]{:S(2)}) %all-to-all-start.9) | async-done | bytes 1572896 | tf_op jit(solution)/shard_map/all_to_all | solution.py:21
  427.1 9.5 %add_bitcast_fusion.2 = f32[1,32,64,256]{3,2,1,0:T(8,128)} fusion(f32[32,64,256]{2,1,0:T(8,128)S(1)} %copy-done.25, bf16[64,32,384]{2,0,1:T(8,128)(2,1)S(1)} %bitcast.291, f32[32,384,256]{2,1,0:T(8,128)} %fusion.74), kind=kOutput, calls=%fused_computation.58 | convolution fusion | flops 431489024 | bytes 18350080 | tf_op jit(solution)/shard_map/ifr,nir->inf/dot_general | solution.py:48
  439.2 47.0 %collective-permute-done.6 = bf16[2048,384]{1,0:T(8,128)(2,1)S(1)} collective-permute-done((bf16[2048,384]{1,0:T(8,128)(2,1)}, bf16[2048,384]{1,0:T(8,128)(2,1)S(1)}, u32[]{:S(2)}, u32[]{:S(2)}) %collective-permute-start.6) | collective-permute-done | bytes 1572896 | tf_op jit(solution)/shard_map/ppermute | solution.py:9
  492.7 4.9 add_bitcast_fusion
  (150 shorter events, 177.6 us)
Async XLA Ops:
  5.5 25.1 %all-to-all-start = ((bf16[16,128,384]{2,0,1:T(8,128)(2,1)}), bf16[16,128,384]{2,0,1:T(8,128)(2,1)}, u32[]{:S(2)}, u32[]{:S(2)}) async-start(bf16[16,128,384]{2,0,1:T(8,128)(2,1)} %copy.78), calls=%async_computation | async-start | bytes 3145728 | tf_op jit(solution)/shard_map/all_to_all | solution.py:17
  12.1 47.4 %copy-start.9 = (bf16[1,1,2048,384]{3,2,1,0:T(8,128)(2,1)}, bf16[1,1,2048,384]{3,2,1,0:T(8,128)(2,1)S(1)}, u32[]{:S(2)}) copy-start(bf16[1,1,2048,384]{3,2,1,0:T(8,128)(2,1)S(1)} %get-tuple-element.43) | copy-start | bytes 4718596
  30.6 24.5 %all-to-all-start.8 = ((bf16[16,128,384]{2,0,1:T(8,128)(2,1)}), bf16[16,128,384]{2,0,1:T(8,128)(2,1)}, u32[]{:S(2)}, u32[]{:S(2)}) async-start(bf16[16,128,384]{2,0,1:T(8,128)(2,1)} %copy.107), calls=%async_computation.8 | async-start | bytes 3145728 | tf_op jit(solution)/shard_map/all_to_all | solution.py:17
  55.1 24.5 %all-to-all-start.1 = ((bf16[64,32,384]{2,1,0:T(8,128)(2,1)}), bf16[64,32,384]{2,1,0:T(8,128)(2,1)}, u32[]{:S(2)}, u32[]{:S(2)}) async-start(bf16[64,32,384]{2,1,0:T(8,128)(2,1)} %copy.81), calls=%async_computation.1 | async-start | bytes 3145728 | tf_op jit(solution)/shard_map/all_to_all | solution.py:21
  79.7 24.7 %all-to-all-start.3 = ((bf16[16,128,384]{2,0,1:T(8,128)(2,1)}), bf16[16,128,384]{2,0,1:T(8,128)(2,1)}, u32[]{:S(2)}, u32[]{:S(2)}) async-start(bf16[16,128,384]{2,0,1:T(8,128)(2,1)} %copy.89), calls=%async_computation.3 | async-start | bytes 3145728 | tf_op jit(solution)/shard_map/all_to_all | solution.py:17
  84.2 105.6 %collective-permute-start.1 = (f32[2048,384]{1,0:T(8,128)}, f32[2048,384]{1,0:T(8,128)}, u32[]{:S(2)}, u32[]{:S(2)}) collective-permute-start(f32[2048,384]{1,0:T(8,128)} %bitcast.278), channel_id=1, source_target_pairs={{0,24},{4,28},{8,0},{12,4},{16,8},{20,12},{24,16},{28,20},{1,25},{... | collective-permute-start | bytes 9437192 | tf_op jit(solution)/shard_map/ppermute | solution.py:9
  88.7 136.6 %collective-permute-start = (f32[2048,384]{1,0:T(8,128)}, f32[2048,384]{1,0:T(8,128)}, u32[]{:S(2)}, u32[]{:S(2)}) collective-permute-start(f32[2048,384]{1,0:T(8,128)} %bitcast.277), channel_id=1, source_target_pairs={{0,8},{4,12},{8,16},{12,20},{16,24},{20,28},{24,0},{28,4},{1,9},{5... | collective-permute-start | bytes 9437192 | tf_op jit(solution)/shard_map/ppermute | solution.py:9
  104.4 24.5 %all-to-all-start.2 = ((bf16[16,128,384]{2,0,1:T(8,128)(2,1)}), bf16[16,128,384]{2,0,1:T(8,128)(2,1)}, u32[]{:S(2)}, u32[]{:S(2)}) async-start(bf16[16,128,384]{2,0,1:T(8,128)(2,1)} %copy.85), calls=%async_computation.2 | async-start | bytes 3145728 | tf_op jit(solution)/shard_map/all_to_all | solution.py:17
  147.4 24.7 %all-to-all-start.4 = ((bf16[64,32,384]{2,1,0:T(8,128)(2,1)}), bf16[64,32,384]{2,1,0:T(8,128)(2,1)}, u32[]{:S(2)}, u32[]{:S(2)}) async-start(bf16[64,32,384]{2,1,0:T(8,128)(2,1)} %copy.92), calls=%async_computation.4 | async-start | bytes 3145728 | tf_op jit(solution)/shard_map/all_to_all | solution.py:21
  172.1 55.8 %all-to-all-start.11 = ((bf16[64,32,384]{2,1,0:T(8,128)(2,1)}), bf16[64,32,384]{2,1,0:T(8,128)(2,1)}, u32[]{:S(2)}, u32[]{:S(2)}) async-start(bf16[64,32,384]{2,1,0:T(8,128)(2,1)} %copy.120), calls=%async_computation.11 | async-start | bytes 3145728 | tf_op jit(solution)/shard_map/all_to_all | solution.py:21
  180.9 79.5 %collective-permute-start.2 = (bf16[2048,384]{1,0:T(8,128)(2,1)}, bf16[2048,384]{1,0:T(8,128)(2,1)}, u32[]{:S(2)}, u32[]{:S(2)}) collective-permute-start(bf16[2048,384]{1,0:T(8,128)(2,1)} %add_convert_fusion.1), channel_id=1, source_target_pairs={{0,4},{4,8},{8,12},{12,16},{16,20},{20,24},{24,28},{28,0},{1,5},{5... | collective-permute-start | bytes 4718600 | tf_op jit(solution)/shard_map/ppermute | solution.py:9
  228.0 38.6 %all-to-all-start.10 = ((bf16[64,32,384]{2,1,0:T(8,128)(2,1)}), bf16[64,32,384]{2,1,0:T(8,128)(2,1)}, u32[]{:S(2)}, u32[]{:S(2)}) async-start(bf16[64,32,384]{2,1,0:T(8,128)(2,1)} %copy.117), calls=%async_computation.10 | async-start | bytes 3145728 | tf_op jit(solution)/shard_map/all_to_all | solution.py:21
  236.6 57.1 %collective-permute-start.3 = (bf16[2048,384]{1,0:T(8,128)(2,1)}, bf16[2048,384]{1,0:T(8,128)(2,1)}, u32[]{:S(2)}, u32[]{:S(2)}) collective-permute-start(bf16[2048,384]{1,0:T(8,128)(2,1)} %add_convert_fusion), channel_id=1, source_target_pairs={{0,28},{4,0},{8,4},{12,8},{16,12},{20,16},{24,20},{28,24},{1,29},{... | collective-permute-start | bytes 4718600 | tf_op jit(solution)/shard_map/ppermute | solution.py:9
  240.1 68.8 %collective-permute-start.5 = (bf16[2048,384]{1,0:T(8,128)(2,1)}, bf16[2048,384]{1,0:T(8,128)(2,1)}, u32[]{:S(2)}, u32[]{:S(2)}) collective-permute-start(bf16[2048,384]{1,0:T(8,128)(2,1)} %convert_element_type.148), channel_id=1, source_target_pairs={{0,24},{4,28},{8,0},{12,4},{16,8},{20,12},{24,16},{28,20},{1,25},{... | collective-permute-start | bytes 4718600 | tf_op jit(solution)/shard_map/ppermute | solution.py:9
  240.6 102.6 %collective-permute-start.4 = (bf16[2048,384]{1,0:T(8,128)(2,1)}, bf16[2048,384]{1,0:T(8,128)(2,1)}, u32[]{:S(2)}, u32[]{:S(2)}) collective-permute-start(bf16[2048,384]{1,0:T(8,128)(2,1)} %convert_element_type.147), channel_id=1, source_target_pairs={{0,8},{4,12},{8,16},{12,20},{16,24},{20,28},{24,0},{28,4},{1,9},{5... | collective-permute-start | bytes 4718600 | tf_op jit(solution)/shard_map/ppermute | solution.py:9
  266.6 82.7 %all-to-all-start.5 = ((bf16[16,128,384]{2,0,1:T(8,128)(2,1)}), bf16[16,128,384]{2,0,1:T(8,128)(2,1)}, u32[]{:S(2)}, u32[]{:S(2)}) async-start(bf16[16,128,384]{2,0,1:T(8,128)(2,1)} %copy.95), calls=%async_computation.5 | async-start | bytes 3145728 | tf_op jit(solution)/shard_map/all_to_all | solution.py:17
  274.0 69.2 %copy-start.17 = (bf16[1,16,128,128]{3,2,1,0:T(8,128)(2,1)S(1)}, bf16[1,16,128,128]{3,2,1,0:T(8,128)(2,1)}, u32[]{:S(2)}) copy-start(bf16[1,16,128,128]{3,2,1,0:T(8,128)(2,1)} %param.13) | copy-start | bytes 1572868
  349.2 24.9 %all-to-all-start.7 = ((bf16[16,128,384]{2,0,1:T(8,128)(2,1)}), bf16[16,128,384]{2,0,1:T(8,128)(2,1)}, u32[]{:S(2)}, u32[]{:S(2)}) async-start(bf16[16,128,384]{2,0,1:T(8,128)(2,1)} %copy.103), calls=%async_computation.7 | async-start | bytes 3145728 | tf_op jit(solution)/shard_map/all_to_all | solution.py:17
  374.1 24.7 %all-to-all-start.6 = ((bf16[64,32,384]{2,1,0:T(8,128)(2,1)}), bf16[64,32,384]{2,1,0:T(8,128)(2,1)}, u32[]{:S(2)}, u32[]{:S(2)}) async-start(bf16[64,32,384]{2,1,0:T(8,128)(2,1)} %copy.99), calls=%async_computation.6 | async-start | bytes 3145728 | tf_op jit(solution)/shard_map/all_to_all | solution.py:21
  398.8 24.5 %all-to-all-start.9 = ((bf16[64,32,384]{2,1,0:T(8,128)(2,1)}), bf16[64,32,384]{2,1,0:T(8,128)(2,1)}, u32[]{:S(2)}, u32[]{:S(2)}) async-start(bf16[64,32,384]{2,1,0:T(8,128)(2,1)} %copy.110), calls=%async_computation.9 | async-start | bytes 3145728 | tf_op jit(solution)/shard_map/all_to_all | solution.py:21
  417.6 68.6 %collective-permute-start.6 = (bf16[2048,384]{1,0:T(8,128)(2,1)}, bf16[2048,384]{1,0:T(8,128)(2,1)S(1)}, u32[]{:S(2)}, u32[]{:S(2)}) collective-permute-start(bf16[2048,384]{1,0:T(8,128)(2,1)} %bitcast.222), channel_id=1, source_target_pairs={{0,4},{4,8},{8,12},{12,16},{16,20},{20,24},{24,28},{28,0},{1,5},{5... | collective-permute-start | bytes 4718600 | tf_op jit(solution)/shard_map/ppermute | solution.py:9
  426.9 65.8 %collective-permute-start.7 = (bf16[2048,384]{1,0:T(8,128)(2,1)}, bf16[2048,384]{1,0:T(8,128)(2,1)}, u32[]{:S(2)}, u32[]{:S(2)}) collective-permute-start(bf16[2048,384]{1,0:T(8,128)(2,1)} %bitcast.69), channel_id=1, source_target_pairs={{0,28},{4,0},{8,4},{12,8},{16,12},{20,16},{24,20},{28,24},{1,29},{... | collective-permute-start | bytes 4718600 | tf_op jit(solution)/shard_map/ppermute | solution.py:9
  439.2 51.4 %copy-start.8 = (bf16[1,1,2048,384]{3,2,1,0:T(8,128)(2,1)S(1)}, bf16[1,1,2048,384]{3,2,1,0:T(8,128)(2,1)}, u32[]{:S(2)}) copy-start(bf16[1,1,2048,384]{3,2,1,0:T(8,128)(2,1)} %copy-done.7) | copy-start | bytes 4718596
  439.2 51.4 %copy-start.24 = (f32[16,128,128]{2,1,0:T(8,128)S(1)}, f32[16,128,128]{2,1,0:T(8,128)}, u32[]{:S(2)}) copy-start(f32[16,128,128]{2,1,0:T(8,128)} %fusion.107) | copy-start | bytes 3145732
  (31 other events, 284.4 us)
where the time goes:
time: 508 us; the launch traced here: 498 us
  waiting for transfers between devices  228 us (45%)
  matrix products  116 us (23%)
  starting transfers between devices  65.9 us (13%)
  local copies, waits for them, and re-layouts  63.2 us (12%)
  other arithmetic  23 us (5%)
    ppermute x8, waiting for transfers between devices, shifted(): lax.ppermute(value, axis, [(i, (i + by) % count) for i in range(count)])  167 us
    all_to_all x6, waiting for transfers between devices, to_rows(): lax.all_to_all(value, 'tensor', split_axis=0, concat_axis=1, tiled=True)  34.6 us
    all_to_all x6, starting transfers between devices, to_columns(): lax.all_to_all(value, 'tensor', split_axis=1, concat_axis=0, tiled=True)  26.8 us
    all_to_all x6, waiting for transfers between devices, to_columns(): lax.all_to_all(value, 'tensor', split_axis=1, concat_axis=0, tiled=True)  26.5 us
    all_to_all x6, starting transfers between devices, to_rows(): lax.all_to_all(value, 'tensor', split_axis=0, concat_axis=1, tiled=True)  26.5 us
    dot_general x4, matrix products, front(): jnp.einsum('ifr,inf->nir', hidden, first_down, preferred_element_type=jnp...  25.2 us
    dot_general x2, matrix products, backward(): jnp.einsum('nir,inf->ifr', grad_folded, first_down, preferred_element_typ...  24.4 us
    dot_general x2, matrix products, backward(): jnp.einsum('ifr,nir->inf', hidden, grad_folded, preferred_element_type=jn...  15.3 us
  transfers between devices with their start and end apart: 20, of which 15 were waited for; matrix products, arithmetic and copies ran while one was open for 38% of the time, Pallas kernels for 0%

commit v1 on v0

--- a/solution.py
+++ b/solution.py
@@ -2,6 +2,7 @@
 import jax.numpy as jnp
 from jax import lax
 from jax.sharding import PartitionSpec as P
+from jax.lax import all_to_all, axis_size
 
 
 def shifted(value, axis, by):
@@ -14,7 +15,15 @@
 
 
 def to_columns(value):
-    return lax.all_to_all(value, "tensor", split_axis=1, concat_axis=0, tiled=True)
+    return jnp.concatenate(
+        all_to_all(
+            jnp.stack(jnp.split(value, axis_size("tensor"), axis=1)),
+            axis_name="tensor",
+            split_axis=0,
+            concat_axis=0,
+        ),
+        0,
+    )
 
 
 def to_rows(value):

time: 508 us -> 466 us (0.917)
  waiting for transfers between devices: 228 us -> 191 us
  local copies, waits for them, and re-layouts: 63.2 us -> 37 us
  starting transfers between devices: 65.9 us -> 75.5 us
  matrix products: 116 us -> 123 us
  other arithmetic: 23 us -> 29.7 us
    ppermute x8, waiting for transfers between devices: 167 us -> 122 us  [shifted(): lax.ppermute(value, axis, [(i, (i + by) % count) for i in range(count)])]
    convert_element_type x6 -> x0, local copies, waits for them, and re-layouts: 14.9 us -> none  [the longest x4 9.09 us: front(): first_out = jnp.einsum('njr,nji->nir', narrow_in, first_up, preferred_ele...]
    all_to_all x6, waiting for transfers between devices: 26.5 us -> 40.1 us  [to_columns(): all_to_all(jnp.stack(jnp.split(value, axis_size('tensor'), axis=1)), axis...]
    all_to_all x6 -> x0, local copies, waits for them, and re-layouts: 12.6 us -> none  [to_columns(): lax.all_to_all(value, 'tensor', split_axis=1, concat_axis=0, tiled=True)]
    ppermute x8, starting transfers between devices: 12.6 us -> 23.8 us  [shifted(): lax.ppermute(value, axis, [(i, (i + by) % count) for i in range(count)])]
    another operation x0 -> x6, other arithmetic: none -> 9.44 us  [to_columns(): jnp.stack(jnp.split(value, axis_size('tensor'), axis=1))]
    all_to_all x6, waiting for transfers between devices: 34.6 us -> 28.7 us  [to_rows(): lax.all_to_all(value, 'tensor', split_axis=0, concat_axis=1, tiled=True)]
where the time goes in v1:
time: 466 us; the launch traced here: 458 us
  waiting for transfers between devices  191 us (41%)
  matrix products  123 us (26%)
  starting transfers between devices  75.5 us (16%)
  local copies, waits for them, and re-layouts  37 us (8%)
  other arithmetic  29.7 us (6%)
    ppermute x8, waiting for transfers between devices, shifted(): lax.ppermute(value, axis, [(i, (i + by) % count) for i in range(count)])  122 us
    all_to_all x6, waiting for transfers between devices, to_columns(): all_to_all(jnp.stack(jnp.split(value, axis_size('tensor'), axis=1)), axis...  40.1 us
    all_to_all x6, waiting for transfers between devices, to_rows(): lax.all_to_all(value, 'tensor', split_axis=0, concat_axis=1, tiled=True)  28.7 us
    dot_general x2, matrix products, backward(): jnp.einsum('nir,inf->ifr', grad_folded, first_down, preferred_element_typ...  27.4 us
    all_to_all x6, starting transfers between devices, to_rows(): lax.all_to_all(value, 'tensor', split_axis=0, concat_axis=1, tiled=True)  26.1 us
    all_to_all x6, starting transfers between devices, to_columns(): all_to_all(jnp.stack(jnp.split(value, axis_size('tensor'), axis=1)), axis...  25.6 us
    dot_general x4, matrix products, front(): jnp.einsum('ifr,inf->nir', hidden, first_down, preferred_element_type=jnp...  25.4 us
    ppermute x8, starting transfers between devices, shifted(): lax.ppermute(value, axis, [(i, (i + by) % count) for i in range(count)])  23.8 us
  transfers between devices with their start and end apart: 20, of which 15 were waited for; matrix products, arithmetic and copies ran while one was open for 38% of the time, Pallas kernels for 0%

profile of v1, /device:TPU:0, one launch (start us, length us, event | category | flops | bytes accessed | tf_op | source)
XLA Modules:
  0.0 457.8 jit_solution(9751749375348364887)
XLA Ops:
  13.7 15.6 %all-to-all-done = bf16[4,16,32,384]{3,2,1,0:T(8,128)(2,1)S(1)} async-done(((bf16[4,16,32,384]{3,2,1,0:T(8,128)(2,1)}), bf16[4,16,32,384]{3,2,1,0:T(8,128)(2,1)S(1)}, u32[]{:S(2)}, u32[]{:S(2)}) %all-to-all-start) | async-done | bytes 1572896 | tf_op jit(solution)/shard_map/all_to_all | solution.py:19
  29.4 7.4 %fusion.61 = bf16[64,32,384]{2,0,1:T(8,128)(2,1)} fusion(bf16[64,32,384]{2,1,0:T(8,128)(2,1)S(1)} %bitcast.307, bf16[1,32,64,256]{3,2,1,0:T(8,128)(2,1)} %param.12, bf16[1,32,64,256]{3,2,1,0:T(8,128)(2,1)S(1)} %copy-done), kind=kOutput, calls=%fused_computation.82 | convolution fusion | flops 834404352 | bytes 5242880 | tf_op jit(solution)/shard_map/ifr,inf->nir/dot_general | solution.py:40
  50.5 13.3 %all-to-all-done.1 = bf16[64,32,384]{2,1,0:T(8,128)(2,1)S(1)} async-done(((bf16[64,32,384]{2,1,0:T(8,128)(2,1)}), bf16[64,32,384]{2,1,0:T(8,128)(2,1)S(1)}, u32[]{:S(2)}, u32[]{:S(2)}) %all-to-all-start.1) | async-done | bytes 1572896 | tf_op jit(solution)/shard_map/all_to_all | solution.py:30
  77.7 10.9 %all-to-all-done.3 = bf16[4,16,32,384]{3,2,1,0:T(8,128)(2,1)S(1)} async-done(((bf16[4,16,32,384]{3,2,1,0:T(8,128)(2,1)}), bf16[4,16,32,384]{3,2,1,0:T(8,128)(2,1)S(1)}, u32[]{:S(2)}, u32[]{:S(2)}) %all-to-all-start.3) | async-done | bytes 1572896 | tf_op jit(solution)/shard_map/all_to_all | solution.py:19
  88.6 4.6 %all-to-all-start.2 = ((bf16[4,16,32,384]{3,2,1,0:T(8,128)(2,1)}), bf16[4,16,32,384]{3,2,1,0:T(8,128)(2,1)}, u32[]{:S(2)}, u32[]{:S(2)}) async-start(bf16[4,16,32,384]{3,2,1,0:T(8,128)(2,1)} %pad_maximum_fusion.1), calls=%async_computation.2 | async-start | bytes 3145728 | tf_op jit(solution)/shard_map/all_to_all | solution.py:19
  95.7 8.8 %fusion.34 = (bf16[32,256,384]{1,2,0:T(8,128)(2,1)}, f32[32,384,256]{2,1,0:T(8,128)}) fusion(bf16[1,32,64,256]{3,2,1,0:T(8,128)(2,1)S(1)} %copy-done, bf16[64,32,384]{2,1,0:T(8,128)(2,1)S(1)} %bitcast.299), kind=kOutput, calls=%fused_computation.45 | convolution fusion | flops 430964736 | bytes 21495808 | tf_op jit(solution)/shard_map/nir,inf->ifr/dot_general | solution.py:38
  104.5 8.8 %all-to-all-done.2 = bf16[4,16,32,384]{3,2,1,0:T(8,128)(2,1)} async-done(((bf16[4,16,32,384]{3,2,1,0:T(8,128)(2,1)}), bf16[4,16,32,384]{3,2,1,0:T(8,128)(2,1)}, u32[]{:S(2)}, u32[]{:S(2)}) %all-to-all-start.2) | async-done | bytes 1572896 | tf_op jit(solution)/shard_map/all_to_all | solution.py:19
  117.7 13.6 %fusion.6 = bf16[32,256,384]{1,2,0:T(8,128)(2,1)S(1)} fusion(f32[32,384,256]{2,1,0:T(8,128)} %get-tuple-element.63, bf16[64,32,384]{2,1,0:T(8,128)(2,1)} %bitcast.24, bf16[1,32,64,256]{3,2,1,0:T(8,128)(2,1)S(1)} %copy-done.27), kind=kOutput, calls=%fused_computation.12 | convolution fusion | flops 465567744 | bytes 21495808 | tf_op jit(solution)/shard_map/nir,inf->ifr/dot_general | solution.py:60
  137.8 4.9 %all-to-all-start.4 = ((bf16[64,32,384]{2,1,0:T(8,128)(2,1)}), bf16[64,32,384]{2,1,0:T(8,128)(2,1)}, u32[]{:S(2)}, u32[]{:S(2)}) async-start(bf16[64,32,384]{2,1,0:T(8,128)(2,1)} %copy.56), calls=%async_computation.4 | async-start | bytes 3145728 | tf_op jit(solution)/shard_map/all_to_all | solution.py:30
  142.8 8.0 %fusion.74 = f32[32,384,256]{2,1,0:T(8,128)} fusion(bf16[64,32,384]{2,1,0:T(8,128)(2,1)} %bitcast.71, bf16[1,32,64,256]{3,2,1,0:T(8,128)(2,1)S(1)} %copy-done), kind=kOutput, calls=%fused_computation.91 | convolution fusion | flops 402653184 | bytes 15204352 | tf_op jit(solution)/shard_map/nir,inf->ifr/dot_general | solution.py:38
  167.2 7.9 %fusion.69 = bf16[64,32,384]{2,0,1:T(8,128)(2,1)S(1)} fusion(bf16[1,32,64,256]{3,2,1,0:T(8,128)(2,1)S(1)} %copy-done.29, f32[32,384,256]{2,1,0:T(8,128)} %fusion.74), kind=kOutput, calls=%fused_computation.86 | convolution fusion | flops 431751168 | bytes 15204352 | tf_op jit(solution)/shard_map/ifr,inf->nir/dot_general | solution.py:40
  181.3 6.1 %all-to-all-done.10 = bf16[64,32,384]{2,1,0:T(8,128)(2,1)} async-done(((bf16[64,32,384]{2,1,0:T(8,128)(2,1)}), bf16[64,32,384]{2,1,0:T(8,128)(2,1)}, u32[]{:S(2)}, u32[]{:S(2)}) %all-to-all-start.10) | async-done | bytes 1572896 | tf_op jit(solution)/shard_map/all_to_all | solution.py:30
  222.8 14.7 %collective-permute-done.4 = bf16[2048,384]{1,0:T(8,128)(2,1)} collective-permute-done((bf16[2048,384]{1,0:T(8,128)(2,1)}, bf16[2048,384]{1,0:T(8,128)(2,1)}, u32[]{:S(2)}, u32[]{:S(2)}) %collective-permute-start.4) | collective-permute-done | bytes 1572896 | tf_op jit(solution)/shard_map/ppermute | solution.py:10
  237.5 33.5 %collective-permute-done.5 = bf16[2048,384]{1,0:T(8,128)(2,1)} collective-permute-done((bf16[2048,384]{1,0:T(8,128)(2,1)}, bf16[2048,384]{1,0:T(8,128)(2,1)}, u32[]{:S(2)}, u32[]{:S(2)}) %collective-permute-start.5) | collective-permute-done | bytes 1572896 | tf_op jit(solution)/shard_map/ppermute | solution.py:10
  271.0 30.9 %collective-permute-done.3 = bf16[2048,384]{1,0:T(8,128)(2,1)} collective-permute-done((bf16[2048,384]{1,0:T(8,128)(2,1)}, bf16[2048,384]{1,0:T(8,128)(2,1)}, u32[]{:S(2)}, u32[]{:S(2)}) %collective-permute-start.3) | collective-permute-done | bytes 1572896 | tf_op jit(solution)/shard_map/ppermute | solution.py:10
  309.8 5.8 %fusion.82 = f32[32,64,256]{2,1,0:T(8,128)} fusion(bf16[32,256,384]{1,2,0:T(8,128)(2,1)} %get-tuple-element.62, bf16[64,32,384]{2,1,0:T(8,128)(2,1)} %bitcast.24), kind=kOutput, calls=%fused_computation.99 | convolution fusion | flops 402653184 | bytes 9961472 | tf_op jit(solution)/shard_map/ifr,nir->inf/dot_general | solution.py:57
  315.6 8.0 %fusion.56 = bf16[64,32,384]{2,0,1:T(8,128)(2,1)} fusion(bf16[64,32,384]{2,1,0:T(8,128)(2,1)} %bitcast.47, bf16[1,32,64,256]{3,2,1,0:T(8,128)(2,1)} %param.12, bf16[1,32,64,256]{3,2,1,0:T(8,128)(2,1)S(1)} %copy-done), kind=kOutput, calls=%fused_computation.81 | convolution fusion | flops 834404352 | bytes 5242880 | tf_op jit(solution)/shard_map/ifr,inf->nir/dot_general | solution.py:40
  330.0 4.6 %all-to-all-start.6 = ((bf16[64,32,384]{2,1,0:T(8,128)(2,1)}), bf16[64,32,384]{2,1,0:T(8,128)(2,1)}, u32[]{:S(2)}, u32[]{:S(2)}) async-start(bf16[64,32,384]{2,1,0:T(8,128)(2,1)} %copy.61), calls=%async_computation.6 | async-start | bytes 3145728 | tf_op jit(solution)/shard_map/all_to_all | solution.py:30
  334.5 13.8 %fusion.13 = bf16[32,256,384]{1,2,0:T(8,128)(2,1)S(1)} fusion(f32[32,384,256]{2,1,0:T(8,128)} %fusion.74, bf16[64,32,384]{2,1,0:T(8,128)(2,1)} %bitcast.64, bf16[1,32,64,256]{3,2,1,0:T(8,128)(2,1)} %param.12), kind=kOutput, calls=%fused_computation.19 | convolution fusion | flops 465567744 | bytes 21495808 | tf_op jit(solution)/shard_map/nir,inf->ifr/dot_general | solution.py:60
  359.0 5.9 %fusion.78 = f32[32,64,256]{2,1,0:T(8,128)} fusion(bf16[32,256,384]{1,2,0:T(8,128)(2,1)} %copy-done.4, bf16[64,32,384]{2,1,0:T(8,128)(2,1)} %bitcast.300), kind=kOutput, calls=%fused_computation.95 | convolution fusion | flops 402653184 | bytes 9961472 | tf_op jit(solution)/shard_map/nir,ifr->inf/dot_general | solution.py:65
  382.7 5.5 %collective-permute-start.7 = (bf16[2048,384]{1,0:T(8,128)(2,1)}, bf16[2048,384]{1,0:T(8,128)(2,1)}, u32[]{:S(2)}, u32[]{:S(2)}) collective-permute-start(bf16[2048,384]{1,0:T(8,128)(2,1)} %bitcast.78), channel_id=1, source_target_pairs={{0,28},{4,0},{8,4},{12,8},{16,12},{20,16},{24,20},{28,24},{1,29},{... | collective-permute-start | bytes 4718600 | tf_op jit(solution)/shard_map/ppermute | solution.py:10
  388.3 10.8 %add_bitcast_fusion.2 = f32[1,32,64,256]{3,2,1,0:T(8,128)} fusion(f32[32,64,256]{2,1,0:T(8,128)S(1)} %copy-done.26, bf16[64,32,384]{2,1,0:T(8,128)(2,1)} %bitcast.64, f32[32,384,256]{2,1,0:T(8,128)} %fusion.74), kind=kOutput, calls=%fused_computation.58 | convolution fusion | flops 431489024 | bytes 18350080 | tf_op jit(solution)/shard_map/ifr,nir->inf/dot_general | solution.py:57
  403.1 42.8 %collective-permute-done.6 = bf16[2048,384]{1,0:T(8,128)(2,1)S(1)} collective-permute-done((bf16[2048,384]{1,0:T(8,128)(2,1)}, bf16[2048,384]{1,0:T(8,128)(2,1)S(1)}, u32[]{:S(2)}, u32[]{:S(2)}) %collective-permute-start.6) | collective-permute-done | bytes 1572896 | tf_op jit(solution)/shard_map/ppermute | solution.py:10
  452.5 4.9 %add_bitcast_fusion = f32[1,2048,384]{2,1,0:T(8,128)} fusion(f32[2048,384]{1,0:T(8,128)} %collective-permute-done.1, bf16[2048,384]{1,0:T(8,128)(2,1)} %collective-permute-done.7, bf16[2048,384]{1,0:T(8,128)(2,1)} %collective-permute-done.5), kind=kLoop, calls=%fused_computation.54 | loop fusion | flops 3145728 | bytes 9437184 | tf_op jit(solution)/shard_map/broadcast_in_dim | solution.py:140
  (148 shorter events, 165.1 us)
Async XLA Ops:
  0.6 28.7 %copy-start = (bf16[1,32,64,256]{3,2,1,0:T(8,128)(2,1)S(1)}, bf16[1,32,64,256]{3,2,1,0:T(8,128)(2,1)}, u32[]{:S(2)}) copy-start(bf16[1,32,64,256]{3,2,1,0:T(8,128)(2,1)} %param.11) | copy-start | bytes 3145732
  5.1 24.3 %all-to-all-start = ((bf16[4,16,32,384]{3,2,1,0:T(8,128)(2,1)}), bf16[4,16,32,384]{3,2,1,0:T(8,128)(2,1)S(1)}, u32[]{:S(2)}, u32[]{:S(2)}) async-start(bf16[4,16,32,384]{3,2,1,0:T(8,128)(2,1)} %pad_maximum_fusion), calls=%async_computation | async-start | bytes 3145728 | tf_op jit(solution)/shard_map/all_to_all | solution.py:19
  9.3 186.9 %collective-permute-start.1 = (f32[2048,384]{1,0:T(8,128)}, f32[2048,384]{1,0:T(8,128)}, u32[]{:S(2)}, u32[]{:S(2)}) collective-permute-start(f32[2048,384]{1,0:T(8,128)} %bitcast.295), channel_id=1, source_target_pairs={{0,24},{4,28},{8,0},{12,4},{16,8},{20,12},{24,16},{28,20},{1,25},{... | collective-permute-start | bytes 9437192 | tf_op jit(solution)/shard_map/ppermute | solution.py:10
  13.7 182.4 %collective-permute-start = (f32[2048,384]{1,0:T(8,128)}, f32[2048,384]{1,0:T(8,128)}, u32[]{:S(2)}, u32[]{:S(2)}) collective-permute-start(f32[2048,384]{1,0:T(8,128)} %bitcast.298), channel_id=1, source_target_pairs={{0,8},{4,12},{8,16},{12,20},{16,24},{20,28},{24,0},{28,4},{1,9},{5... | collective-permute-start | bytes 9437192 | tf_op jit(solution)/shard_map/ppermute | solution.py:10
  40.2 23.6 %all-to-all-start.1 = ((bf16[64,32,384]{2,1,0:T(8,128)(2,1)}), bf16[64,32,384]{2,1,0:T(8,128)(2,1)S(1)}, u32[]{:S(2)}, u32[]{:S(2)}) async-start(bf16[64,32,384]{2,1,0:T(8,128)(2,1)} %copy.49), calls=%async_computation.1 | async-start | bytes 3145728 | tf_op jit(solution)/shard_map/all_to_all | solution.py:30
  65.0 23.6 %all-to-all-start.3 = ((bf16[4,16,32,384]{3,2,1,0:T(8,128)(2,1)}), bf16[4,16,32,384]{3,2,1,0:T(8,128)(2,1)S(1)}, u32[]{:S(2)}, u32[]{:S(2)}) async-start(bf16[4,16,32,384]{3,2,1,0:T(8,128)(2,1)} %pad_maximum_fusion.2), calls=%async_computation.3 | async-start | bytes 3145728 | tf_op jit(solution)/shard_map/all_to_all | solution.py:19
  88.6 24.7 %all-to-all-start.2 = ((bf16[4,16,32,384]{3,2,1,0:T(8,128)(2,1)}), bf16[4,16,32,384]{3,2,1,0:T(8,128)(2,1)}, u32[]{:S(2)}, u32[]{:S(2)}) async-start(bf16[4,16,32,384]{3,2,1,0:T(8,128)(2,1)} %pad_maximum_fusion.1), calls=%async_computation.2 | async-start | bytes 3145728 | tf_op jit(solution)/shard_map/all_to_all | solution.py:19
  113.3 24.5 %all-to-all-start.8 = ((bf16[4,16,32,384]{3,2,1,0:T(8,128)(2,1)}), bf16[4,16,32,384]{3,2,1,0:T(8,128)(2,1)}, u32[]{:S(2)}, u32[]{:S(2)}) async-start(bf16[4,16,32,384]{3,2,1,0:T(8,128)(2,1)} %pad_maximum_fusion.5), calls=%async_computation.8 | async-start | bytes 3145728 | tf_op jit(solution)/shard_map/all_to_all | solution.py:19
  137.8 25.0 %all-to-all-start.4 = ((bf16[64,32,384]{2,1,0:T(8,128)(2,1)}), bf16[64,32,384]{2,1,0:T(8,128)(2,1)}, u32[]{:S(2)}, u32[]{:S(2)}) async-start(bf16[64,32,384]{2,1,0:T(8,128)(2,1)} %copy.56), calls=%async_computation.4 | async-start | bytes 3145728 | tf_op jit(solution)/shard_map/all_to_all | solution.py:30
  156.4 49.7 %collective-permute-start.2 = (bf16[2048,384]{1,0:T(8,128)(2,1)}, bf16[2048,384]{1,0:T(8,128)(2,1)}, u32[]{:S(2)}, u32[]{:S(2)}) collective-permute-start(bf16[2048,384]{1,0:T(8,128)(2,1)} %add_convert_fusion.1), channel_id=1, source_target_pairs={{0,4},{4,8},{8,12},{12,16},{16,20},{20,24},{24,28},{28,0},{1,5},{5... | collective-permute-start | bytes 4718600 | tf_op jit(solution)/shard_map/ppermute | solution.py:10
  162.9 24.5 %all-to-all-start.10 = ((bf16[64,32,384]{2,1,0:T(8,128)(2,1)}), bf16[64,32,384]{2,1,0:T(8,128)(2,1)}, u32[]{:S(2)}, u32[]{:S(2)}) async-start(bf16[64,32,384]{2,1,0:T(8,128)(2,1)} %copy.79), calls=%async_computation.10 | async-start | bytes 3145728 | tf_op jit(solution)/shard_map/all_to_all | solution.py:30
  187.4 24.5 %all-to-all-start.11 = ((bf16[64,32,384]{2,1,0:T(8,128)(2,1)}), bf16[64,32,384]{2,1,0:T(8,128)(2,1)}, u32[]{:S(2)}, u32[]{:S(2)}) async-start(bf16[64,32,384]{2,1,0:T(8,128)(2,1)} %copy.82), calls=%async_computation.11 | async-start | bytes 3145728 | tf_op jit(solution)/shard_map/all_to_all | solution.py:30
  197.5 40.0 %collective-permute-start.4 = (bf16[2048,384]{1,0:T(8,128)(2,1)}, bf16[2048,384]{1,0:T(8,128)(2,1)}, u32[]{:S(2)}, u32[]{:S(2)}) collective-permute-start(bf16[2048,384]{1,0:T(8,128)(2,1)} %convert_element_type.147), channel_id=1, source_target_pairs={{0,8},{4,12},{8,16},{12,20},{16,24},{20,28},{24,0},{28,4},{1,9},{5... | collective-permute-start | bytes 4718600 | tf_op jit(solution)/shard_map/ppermute | solution.py:10
  201.2 69.8 %collective-permute-start.5 = (bf16[2048,384]{1,0:T(8,128)(2,1)}, bf16[2048,384]{1,0:T(8,128)(2,1)}, u32[]{:S(2)}, u32[]{:S(2)}) collective-permute-start(bf16[2048,384]{1,0:T(8,128)(2,1)} %convert_element_type.148), channel_id=1, source_target_pairs={{0,24},{4,28},{8,0},{12,4},{16,8},{20,12},{24,16},{28,20},{1,25},{... | collective-permute-start | bytes 4718600 | tf_op jit(solution)/shard_map/ppermute | solution.py:10
  204.3 97.6 %collective-permute-start.3 = (bf16[2048,384]{1,0:T(8,128)(2,1)}, bf16[2048,384]{1,0:T(8,128)(2,1)}, u32[]{:S(2)}, u32[]{:S(2)}) collective-permute-start(bf16[2048,384]{1,0:T(8,128)(2,1)} %add_convert_fusion), channel_id=1, source_target_pairs={{0,28},{4,0},{8,4},{12,8},{16,12},{20,16},{24,20},{28,24},{1,29},{... | collective-permute-start | bytes 4718600 | tf_op jit(solution)/shard_map/ppermute | solution.py:10
  211.8 93.6 %all-to-all-start.5 = ((bf16[4,16,32,384]{3,2,1,0:T(8,128)(2,1)}), bf16[4,16,32,384]{3,2,1,0:T(8,128)(2,1)}, u32[]{:S(2)}, u32[]{:S(2)}) async-start(bf16[4,16,32,384]{3,2,1,0:T(8,128)(2,1)} %pad_maximum_fusion.3), calls=%async_computation.5 | async-start | bytes 3145728 | tf_op jit(solution)/shard_map/all_to_all | solution.py:19
  221.0 80.8 %copy-start.17 = (bf16[1,16,128,128]{3,2,1,0:T(8,128)(2,1)S(1)}, bf16[1,16,128,128]{3,2,1,0:T(8,128)(2,1)}, u32[]{:S(2)}) copy-start(bf16[1,16,128,128]{3,2,1,0:T(8,128)(2,1)} %param.13) | copy-start | bytes 1572868
  305.5 24.5 %all-to-all-start.7 = ((bf16[4,16,32,384]{3,2,1,0:T(8,128)(2,1)}), bf16[4,16,32,384]{3,2,1,0:T(8,128)(2,1)}, u32[]{:S(2)}, u32[]{:S(2)}) async-start(bf16[4,16,32,384]{3,2,1,0:T(8,128)(2,1)} %pad_maximum_fusion.4), calls=%async_computation.7 | async-start | bytes 3145728 | tf_op jit(solution)/shard_map/all_to_all | solution.py:19
  330.0 24.7 %all-to-all-start.6 = ((bf16[64,32,384]{2,1,0:T(8,128)(2,1)}), bf16[64,32,384]{2,1,0:T(8,128)(2,1)}, u32[]{:S(2)}, u32[]{:S(2)}) async-start(bf16[64,32,384]{2,1,0:T(8,128)(2,1)} %copy.61), calls=%async_computation.6 | async-start | bytes 3145728 | tf_op jit(solution)/shard_map/all_to_all | solution.py:30
  354.7 24.5 %all-to-all-start.9 = ((bf16[64,32,384]{2,1,0:T(8,128)(2,1)}), bf16[64,32,384]{2,1,0:T(8,128)(2,1)}, u32[]{:S(2)}, u32[]{:S(2)}) async-start(bf16[64,32,384]{2,1,0:T(8,128)(2,1)} %copy.68), calls=%async_computation.9 | async-start | bytes 3145728 | tf_op jit(solution)/shard_map/all_to_all | solution.py:30
  373.4 72.5 %collective-permute-start.6 = (bf16[2048,384]{1,0:T(8,128)(2,1)}, bf16[2048,384]{1,0:T(8,128)(2,1)S(1)}, u32[]{:S(2)}, u32[]{:S(2)}) collective-permute-start(bf16[2048,384]{1,0:T(8,128)(2,1)} %bitcast.252), channel_id=1, source_target_pairs={{0,4},{4,8},{8,12},{12,16},{16,20},{20,24},{24,28},{28,0},{1,5},{5... | collective-permute-start | bytes 4718600 | tf_op jit(solution)/shard_map/ppermute | solution.py:10
  382.7 69.7 %collective-permute-start.7 = (bf16[2048,384]{1,0:T(8,128)(2,1)}, bf16[2048,384]{1,0:T(8,128)(2,1)}, u32[]{:S(2)}, u32[]{:S(2)}) collective-permute-start(bf16[2048,384]{1,0:T(8,128)(2,1)} %bitcast.78), channel_id=1, source_target_pairs={{0,28},{4,0},{8,4},{12,8},{16,12},{20,16},{24,20},{28,24},{1,29},{... | collective-permute-start | bytes 4718600 | tf_op jit(solution)/shard_map/ppermute | solution.py:10
  403.1 47.2 %copy-start.9 = (bf16[1,1,2048,384]{3,2,1,0:T(8,128)(2,1)S(1)}, bf16[1,1,2048,384]{3,2,1,0:T(8,128)(2,1)}, u32[]{:S(2)}) copy-start(bf16[1,1,2048,384]{3,2,1,0:T(8,128)(2,1)} %copy-done.8) | copy-start | bytes 4718596
  403.1 47.2 %copy-start.25 = (f32[16,128,128]{2,1,0:T(8,128)S(1)}, f32[16,128,128]{2,1,0:T(8,128)}, u32[]{:S(2)}) copy-start(f32[16,128,128]{2,1,0:T(8,128)} %fusion.125) | copy-start | bytes 3145732
  (30 other events, 170.2 us)
